TPU v7x, 256 devices: a whole 4x4x8 slice. The times are simulated.
256 devices in a mesh: gx: 16 (over z, core), gy: 16 (over y, x).
Axes of the slice: x: 4, y: 4, z: 8, core: 2. Of those that a mesh axis runs over, the one named last changes fastest.
Arguments:
- field: float32 [64, 4096, 128], P('gy', 'gx'), may hold values from -5 to 5
- courant: float32 [3, 64, 4096, 128], P(None, 'gy', 'gx'), may hold values from -2.5 to 2.5
- diffusion_number: float32 [64, 4096, 128], P('gy', 'gx'), may hold values from 65536 to 1310720
Outputs:
- solved: float32 [64, 4096, 128], P('gy', 'gx')
All inputs are finite; a program needn't handle non-finite values.
Results may differ from a plain program's by a relative error of at most 0.0013.
Values sent between devices are 32-bit elements; how exact they have to be, the bound alone decides.
No kernel may reach another device: no remote copies, remote signals or barrier semaphores. Data moves between devices by JAX's collectives and lax.ppermute only.
A program may use at most 64 MiB of HBM per device.

v0:
```python
import jax
import jax.numpy as jnp
from jax import lax
from jax.sharding import PartitionSpec as P


def padded_2(cells, sides, width, closed):
    for axis, dim in sides:
        count = lax.axis_size(axis)
        ends = count if closed else count - 1
        head = lax.slice_in_dim(cells, 0, width, axis=dim)
        tail = lax.slice_in_dim(cells, cells.shape[dim] - width, cells.shape[dim], axis=dim)
        cells = jnp.concatenate(
            [
                lax.ppermute(tail, axis, [(i, (i + 1) % count) for i in range(ends)]),
                cells,
                lax.ppermute(head, axis, [((i + 1) % count, i) for i in range(ends)]),
            ],
            axis=dim,
        )
    return cells


def difference_pair(padded, sweep_direction, length):
    shifted = [
        lax.slice_in_dim(padded, offset, offset + length, axis=sweep_direction)
        for offset in range(5)
    ]
    gradient = (8.0 * (shifted[3] - shifted[1]) - (shifted[4] - shifted[0])) / 12.0
    curvature = (
        16.0 * (shifted[3] + shifted[1]) - (shifted[4] + shifted[0]) - 30.0 * shifted[2]
    ) / 12.0
    return (gradient, curvature)


def build_rhs(field, courant, y_padded, x_padded):
    z_padded = jnp.concatenate([field[:, :, -2:], field, field[:, :, :2]], 2)
    grad_y, curve_y = difference_pair(y_padded, 0, field.shape[0])
    grad_x = difference_pair(x_padded, 1, field.shape[1])[0]
    grad_z, curve_z = difference_pair(z_padded, 2, field.shape[2])
    transport = courant[0] * grad_x + courant[1] * grad_y + courant[2] * grad_z
    return field - transport + 0.05 * (curve_y + curve_z) + 0.3 * field / (1.0 + field * field)


def rows_below(values, stride, fill, sweep_direction):
    length = values.shape[sweep_direction]
    filler = jnp.full_like(lax.slice_in_dim(values, 0, stride, axis=sweep_direction), fill)
    return jnp.concatenate(
        [filler, lax.slice_in_dim(values, 0, length - stride, axis=sweep_direction)],
        sweep_direction,
    )


def rows_above(values, stride, fill, sweep_direction):
    length = values.shape[sweep_direction]
    filler = jnp.full_like(
        lax.slice_in_dim(values, length - stride, length, axis=sweep_direction), fill
    )
    return jnp.concatenate(
        [lax.slice_in_dim(values, stride, length, axis=sweep_direction), filler], sweep_direction
    )


def combine_rows(own_rows, below_set, above_set):
    lower_band, main_diagonal, upper_band, right_hand_sides = own_rows
    low_sub, low_diag, low_super, low_rights = below_set
    high_sub, high_diag, high_super, high_rights = above_set
    factor_low = -lower_band / low_diag
    factor_high = -upper_band / high_diag
    new_sub = factor_low * low_sub
    new_super = factor_high * high_super
    new_diag = main_diagonal + factor_low * low_super + factor_high * high_sub
    new_rights = tuple(
        (
            value + factor_low * lower_value + factor_high * upper_value
            for value, lower_value, upper_value in zip(right_hand_sides, low_rights, high_rights)
        )
    )
    return (new_sub, new_diag, new_super, new_rights)


def parallel_cyclic_reduction(
    lower_band, main_diagonal, upper_band, right_hand_sides, sweep_direction
):
    length = main_diagonal.shape[sweep_direction]
    stride = 1
    while stride < length:
        below_set = (
            rows_below(lower_band, stride, 0.0, sweep_direction),
            rows_below(main_diagonal, stride, 1.0, sweep_direction),
            rows_below(upper_band, stride, 0.0, sweep_direction),
            tuple((rows_below(value, stride, 0.0, sweep_direction) for value in right_hand_sides)),
        )
        above_set = (
            rows_above(lower_band, stride, 0.0, sweep_direction),
            rows_above(main_diagonal, stride, 1.0, sweep_direction),
            rows_above(upper_band, stride, 0.0, sweep_direction),
            tuple((rows_above(value, stride, 0.0, sweep_direction) for value in right_hand_sides)),
        )
        lower_band, main_diagonal, upper_band, right_hand_sides = combine_rows(
            (lower_band, main_diagonal, upper_band, right_hand_sides), below_set, above_set
        )
        stride = stride * 2
    return tuple((value / main_diagonal for value in right_hand_sides))


def shards(field, courant, diffusion_number):
    y_padded = padded_2(field, (("gy", 0),), 2, True)
    x_padded = padded_2(field, (("gx", 1),), 2, False)
    rhs = build_rhs(field, courant, y_padded, x_padded)
    place = lax.axis_index("gx")
    device_count = lax.axis_size("gx")
    sub_full = -diffusion_number
    diag_full = 1.0 + 2.0 * diffusion_number
    super_full = -diffusion_number
    edge_zeros = jnp.zeros_like(rhs[:, 0:1])
    inner_zeros = jnp.zeros_like(rhs[:, 3:])
    sub_inner = jnp.concatenate([edge_zeros, sub_full[:, 2:-1]], 1)
    super_inner = jnp.concatenate([super_full[:, 1:-2], edge_zeros], 1)
    diag_inner = diag_full[:, 1:-1]
    first_unit = jnp.concatenate([-sub_full[:, 1:2], inner_zeros], 1)
    last_unit = jnp.concatenate([inner_zeros, -super_full[:, -2:-1]], 1)
    particular_solution, first_row_response, last_row_response = parallel_cyclic_reduction(
        sub_inner, diag_inner, super_inner, (rhs[:, 1:-1], first_unit, last_unit), 1
    )
    low_open = (place > 0).astype(jnp.float32)
    high_open = (place < device_count - 1).astype(jnp.float32)
    sub_first = sub_full[:, 0:1] * low_open
    diag_first = diag_full[:, 0:1] + super_full[:, 0:1] * first_row_response[:, 0:1]
    super_first = super_full[:, 0:1] * last_row_response[:, 0:1]
    right_first = rhs[:, 0:1] - super_full[:, 0:1] * particular_solution[:, 0:1]
    sub_last = sub_full[:, -1:] * first_row_response[:, -1:]
    diag_last = diag_full[:, -1:] + sub_full[:, -1:] * last_row_response[:, -1:]
    super_last = super_full[:, -1:] * high_open
    right_last = rhs[:, -1:] - sub_full[:, -1:] * particular_solution[:, -1:]
    reduced_sub = jnp.concatenate([sub_first, sub_last], 1)
    reduced_diag = jnp.concatenate([diag_first, diag_last], 1)
    reduced_super = jnp.concatenate([super_first, super_last], 1)
    reduced_right = jnp.concatenate([right_first, right_last], 1)
    stacked = jnp.concatenate([reduced_sub, reduced_diag, reduced_super, reduced_right], 1)
    gathered = lax.all_gather(stacked, "gx", axis=1, tiled=True)
    gathered = gathered.reshape(gathered.shape[0], device_count, 4, 2, gathered.shape[-1])
    gathered_lower_band, gathered_diagonal, gathered_upper_band, gathered_rhs = (
        gathered[:, :, k].reshape(gathered.shape[0], 2 * device_count, gathered.shape[-1])
        for k in range(4)
    )
    boundary_rows_gathered = parallel_cyclic_reduction(
        gathered_lower_band, gathered_diagonal, gathered_upper_band, (gathered_rhs,), 1
    )[0]
    ends = lax.dynamic_slice_in_dim(boundary_rows_gathered, 2 * place, 2, 1)
    interior = (
        particular_solution + first_row_response * ends[:, 0:1] + last_row_response * ends[:, 1:2]
    )
    return jnp.concatenate([ends[:, 0:1], interior, ends[:, 1:2]], 1)


def solution(mesh):
    in_specs = (P("gy", "gx", None), P(None, "gy", "gx", None), P("gy", "gx", None))
    out_specs = P("gy", "gx", None)
    return jax.shard_map(shards, mesh=mesh, in_specs=in_specs, out_specs=out_specs, check_vma=False)
```

profile of v0, /device:TPU:1, one launch (start us, length us, event | category | flops | bytes accessed | tf_op | source)
XLA Modules:
  0.0 54.8 jit_solution(11624598500980363579)
XLA Ops:
  0.0 1.9 %fusion.76 = (f32[2,256,128]{2,1,0:T(8,128)}, f32[2,256,128]{2,1,0:T(8,128)}) fusion(f32[4,256,128]{2,1,0:T(8,128)} %param.3), kind=kLoop, calls=%fused_computation.204 | loop fusion | bytes 1048576 | tf_op jit(solution)/shard_map/slice | solution.py:11
  1.9 2.0 %collective-permute-start.3 = (f32[2,256,128]{2,1,0:T(8,128)}, f32[2,256,128]{2,1,0:T(8,128)}, u32[]{:S(2)}, u32[]{:S(2)}) collective-permute-start(f32[2,256,128]{2,1,0:T(8,128)} %get-tuple-element.169), channel_id=1, source_target_pairs={{0,1},{1,2},{2,3},{3,4},{4,5},{5,6},{6,7},{7,8},{8,9},{9,10},{10,1... | collective-permute-start | bytes 786440 | tf_op jit(solution)/shard_map/ppermute | solution.py:15
  3.9 3.7 %collective-permute-start.2 = (f32[2,256,128]{2,1,0:T(8,128)}, f32[2,256,128]{2,1,0:T(8,128)S(1)}, u32[]{:S(2)}, u32[]{:S(2)}) collective-permute-start(f32[2,256,128]{2,1,0:T(8,128)} %get-tuple-element.168), channel_id=1, source_target_pairs={{1,0},{2,1},{3,2},{4,3},{5,4},{6,5},{7,6},{8,7},{9,8},{10,9},{11,1... | collective-permute-start | bytes 786440 | tf_op jit(solution)/shard_map/ppermute | solution.py:17
  7.6 0.7 %fusion.78 = (f32[4,2,128]{2,1,0:T(2,128)S(1)}, f32[4,2,128]{2,1,0:T(2,128)S(1)}) fusion(f32[4,256,128]{2,1,0:T(8,128)} %param.3), kind=kLoop, calls=%fused_computation.206 | loop fusion | bytes 16384 | tf_op jit(solution)/shard_map/slice | solution.py:11
  8.4 4.7 %collective-permute-start = (f32[4,2,128]{2,1,0:T(2,128)S(1)}, f32[4,2,128]{2,1,0:T(2,128)S(1)}, u32[]{:S(2)}, u32[]{:S(2)}) collective-permute-start(f32[4,2,128]{2,1,0:T(2,128)S(1)} %get-tuple-element.175), channel_id=1, source_target_pairs={{16,0},{32,16},{48,32},{64,48},{80,64},{96,80},{112,96},{128,112},... | collective-permute-start | bytes 12296 | tf_op jit(solution)/shard_map/ppermute | solution.py:17
  13.1 1.9 %collective-permute-start.1 = (f32[4,2,128]{2,1,0:T(2,128)S(1)}, f32[4,2,128]{2,1,0:T(2,128)S(1)}, u32[]{:S(2)}, u32[]{:S(2)}) collective-permute-start(f32[4,2,128]{2,1,0:T(2,128)S(1)} %get-tuple-element.176), channel_id=1, source_target_pairs={{0,16},{16,32},{32,48},{48,64},{64,80},{80,96},{96,112},{112,128},... | collective-permute-start | bytes 12296 | tf_op jit(solution)/shard_map/ppermute | solution.py:15
  15.0 1.1 %multiply_add_fusion.26 = (f32[4,256,128]{2,1,0:T(8,128)S(1)}, f32[4,256,128]{2,1,0:T(8,128)S(1)}) fusion(f32[4,256,128]{2,1,0:T(8,128)} %param.5), kind=kLoop, calls=%fused_computation.95 | loop fusion | flops 393216 | bytes 1572864 | tf_op jit(solution)/shard_map/add | solution.py:114
  16.1 1.2 %fusion.73 = (f32[4,253,128]{2,1,0:T(8,128)S(1)}, f32[4,253,128]{2,1,0:T(8,128)S(1)}, f32[4,253,128]{2,1,0:T(8,128)}, f32[4,253,128]{2,1,0:T(8,128)}) fusion(f32[4,256,128]{2,1,0:T(8,128)S(1)} %get-tuple-element.165, f32[4,256,128]{2,1,0:T(8,128)S(1)} %get-tuple-element.164), kind=kLoop, calls=%fused_computation.201 | loop fusion | bytes 4145152 | tf_op jit(solution)/shard_map/slice | solution.py:119
  17.4 0.8 %pad_slice_fusion.9 = f32[4,253,128]{2,1,0:T(8,128)} fusion(f32[4,253,128]{2,1,0:T(8,128)S(1)} %get-tuple-element.161), kind=kLoop, calls=%fused_computation.97 | loop fusion | bytes 1036288 | tf_op jit(solution)/shard_map/slice | solution.py:49
  18.3 1.1 %pad_slice_fusion.4 = (f32[4,253,128]{2,1,0:T(8,128)}, f32[4,253,128]{2,1,0:T(8,128)}) fusion(f32[4,1,128]{2,1,0:T(1,128)S(1)} %get-tuple-element.93, f32[4,1,128]{2,1,0:T(1,128)S(1)} %get-tuple-element.94), kind=kLoop, calls=%fused_computation.4 | loop fusion | bytes 1040384 | tf_op jit(solution)/shard_map/slice | solution.py:60
  19.5 1.1 %constant_dynamic-update-slice_fusion.5 = f32[6,256,128]{2,1,0:T(8,128)S(1)} fusion(f32[2,256,128]{2,1,0:T(8,128)} %collective-permute-done.3), kind=kLoop, calls=%fused_computation.133 | loop fusion | bytes 524288
  21.0 1.2 %fusion.10 = f32[4,256,128]{2,1,0:T(8,128)S(1)} fusion(f32[4,256,128]{2,1,0:T(8,128)S(1)} %copy-done, f32[4,2,128]{2,1,0:T(2,128)S(1)} %collective-permute-done.1, f32[4,258,128]{2,1,0:T(8,128)S(1)} %constant_dynamic-update-slice_fusion, f32[4,256,2]{2,1,0:T(8,128)S(1)} %get-tuple-element.174, f32[4,256,2]{2,1,0:T(8,128)S(1)} %get-tuple-element.173, ...), kind=kLoop, calls=%fused_computation.20 | loop fusion | flops 6029312 | bytes 5787648 | tf_op jit(solution)/shard_map/add | solution.py:42
  22.3 0.9 %copy-done.4 = f32[4,253,128]{2,1,0:T(8,128)S(1)} copy-done((f32[4,253,128]{2,1,0:T(8,128)S(1)}, f32[4,253,128]{2,1,0:T(8,128)}, u32[]{:S(2)}) %copy-start.4) | copy-done | bytes 518168
  24.1 0.9 %copy-done.1 = f32[4,253,128]{2,1,0:T(8,128)S(1)} copy-done((f32[4,253,128]{2,1,0:T(8,128)S(1)}, f32[4,253,128]{2,1,0:T(8,128)}, u32[]{:S(2)}) %copy-start.1) | copy-done | bytes 518168
  25.3 0.6 %multiply_add_fusion.6 = (f32[4,254,128]{2,1,0:T(8,128)S(1)}, f32[4,254,128]{2,1,0:T(8,128)S(1)}, f32[4,254,128]{2,1,0:T(8,128)S(1)}, f32[4,254,128]{2,1,0:T(8,1...) fusion(f32[4,252,128]{2,1,0:T(8,128)S(1)} %get-tuple-element.159, ...), kind=kLoop, calls=%fused_computation.43 | loop fusion | flops 2340864 | bytes 9343992 | tf_op jit(solution)/shard_map/add | solution.py:75
  26.5 0.9 %multiply_add_fusion.5 = (f32[4,254,128]{2,1,0:T(8,128)S(1)}, f32[4,254,128]{2,1,0:T(8,128)S(1)}, f32[4,254,128]{2,1,0:T(8,128)S(1)}, f32[4,254,128]{2,1,0:T(8,1...) fusion(f32[4,250,128]{2,1,0:T(8,128)S(1)} %get-tuple-element.155, ...), kind=kLoop, calls=%fused_computation.42 | loop fusion | flops 2340864 | bytes 11386880 | tf_op jit(solution)/shard_map/add | solution.py:75
  28.0 0.7 %multiply_add_fusion.4 = (f32[4,254,128]{2,1,0:T(8,128)S(1)}, f32[4,254,128]{2,1,0:T(8,128)S(1)}, f32[4,254,128]{2,1,0:T(8,128)S(1)}, f32[4,254,128]{2,1,0:T(8,1...) fusion(f32[4,246,128]{2,1,0:T(8,128)S(1)} %get-tuple-element.147, ...), kind=kLoop, calls=%fused_computation.41 | loop fusion | flops 2340864 | bytes 11329536 | tf_op jit(solution)/shard_map/add | solution.py:75
  29.3 0.4 multiply_add_fusion.3
  30.3 0.5 multiply_add_fusion.2
  31.4 0.5 multiply_add_fusion.1
  32.2 0.4 multiply_add_fusion.7
  33.1 0.4 add_divide_fusion
  33.6 19.3 %all_gather.3 = f32[4,128,128]{2,1,0:T(8,128)S(1)} all-gather(f32[4,8,128]{2,1,0:T(8,128)S(1)} %concatenate.548), channel_id=1, replica_groups=mesh['gx'=16,'gy'=16] {'gx'}, dimensions={1}, use_global_device_ids=true | all-gather | bytes 278528 | tf_op jit(solution)/shard_map/all_gather | solution.py:141
  54.0 0.8 %pad_maximum_fusion.3 = f32[4,256,128]{2,1,0:T(8,128)} fusion(f32[4,1,128]{2,1,0:T(1,128)S(1)} %get-tuple-element.223, f32[4,254,128]{2,1,0:T(8,128)S(1)} %multiply_add_fusion, f32[4,1,128]{2,1,0:T(1,128)S(1)} %get-tuple-element.222), kind=kLoop, calls=%fused_computation.33 | loop fusion | flops 262144 | bytes 1048576 | tf_op jit(solution)/shard_map/concatenate | solution.py:154
  (108 shorter events, 6.2 us)
Async XLA Ops:
  1.9 17.7 %collective-permute-start.3 = (f32[2,256,128]{2,1,0:T(8,128)}, f32[2,256,128]{2,1,0:T(8,128)}, u32[]{:S(2)}, u32[]{:S(2)}) collective-permute-start(f32[2,256,128]{2,1,0:T(8,128)} %get-tuple-element.169), channel_id=1, source_target_pairs={{0,1},{1,2},{2,3},{3,4},{4,5},{5,6},{6,7},{7,8},{8,9},{9,10},{10,1... | collective-permute-start | bytes 786440 | tf_op jit(solution)/shard_map/ppermute | solution.py:15
  3.9 16.8 %collective-permute-start.2 = (f32[2,256,128]{2,1,0:T(8,128)}, f32[2,256,128]{2,1,0:T(8,128)S(1)}, u32[]{:S(2)}, u32[]{:S(2)}) collective-permute-start(f32[2,256,128]{2,1,0:T(8,128)} %get-tuple-element.168), channel_id=1, source_target_pairs={{1,0},{2,1},{3,2},{4,3},{5,4},{6,5},{7,6},{8,7},{9,8},{10,9},{11,1... | collective-permute-start | bytes 786440 | tf_op jit(solution)/shard_map/ppermute | solution.py:17
  8.4 12.4 %collective-permute-start = (f32[4,2,128]{2,1,0:T(2,128)S(1)}, f32[4,2,128]{2,1,0:T(2,128)S(1)}, u32[]{:S(2)}, u32[]{:S(2)}) collective-permute-start(f32[4,2,128]{2,1,0:T(2,128)S(1)} %get-tuple-element.175), channel_id=1, source_target_pairs={{16,0},{32,16},{48,32},{64,48},{80,64},{96,80},{112,96},{128,112},... | collective-permute-start | bytes 12296 | tf_op jit(solution)/shard_map/ppermute | solution.py:17
  13.1 7.7 %collective-permute-start.1 = (f32[4,2,128]{2,1,0:T(2,128)S(1)}, f32[4,2,128]{2,1,0:T(2,128)S(1)}, u32[]{:S(2)}, u32[]{:S(2)}) collective-permute-start(f32[4,2,128]{2,1,0:T(2,128)S(1)} %get-tuple-element.176), channel_id=1, source_target_pairs={{0,16},{16,32},{32,48},{48,64},{64,80},{80,96},{96,112},{112,128},... | collective-permute-start | bytes 12296 | tf_op jit(solution)/shard_map/ppermute | solution.py:15
  17.4 2.0 %copy-start = (f32[4,256,128]{2,1,0:T(8,128)S(1)}, f32[4,256,128]{2,1,0:T(8,128)}, u32[]{:S(2)}) copy-start(f32[4,256,128]{2,1,0:T(8,128)} %param.3) | copy-start | bytes 1572868
  19.5 1.5 %copy-start.6 = (f32[3,4,256,128]{3,2,1,0:T(8,128)S(1)}, f32[3,4,256,128]{3,2,1,0:T(8,128)}, u32[]{:S(2)}) copy-start(f32[3,4,256,128]{3,2,1,0:T(8,128)} %param.4) | copy-start | bytes 4718596
  22.2 1.0 %copy-start.4 = (f32[4,253,128]{2,1,0:T(8,128)S(1)}, f32[4,253,128]{2,1,0:T(8,128)}, u32[]{:S(2)}) copy-start(f32[4,253,128]{2,1,0:T(8,128)} %get-tuple-element.224) | copy-start | bytes 1554436
  22.2 1.2 %copy-start.5 = (f32[4,253,128]{2,1,0:T(8,128)S(1)}, f32[4,253,128]{2,1,0:T(8,128)}, u32[]{:S(2)}) copy-start(f32[4,253,128]{2,1,0:T(8,128)} %get-tuple-element.225) | copy-start | bytes 1554436
  24.0 1.0 %copy-start.1 = (f32[4,253,128]{2,1,0:T(8,128)S(1)}, f32[4,253,128]{2,1,0:T(8,128)}, u32[]{:S(2)}) copy-start(f32[4,253,128]{2,1,0:T(8,128)} %pad_slice_fusion.9) | copy-start | bytes 1554436
  24.0 1.2 %copy-start.2 = (f32[4,253,128]{2,1,0:T(8,128)S(1)}, f32[4,253,128]{2,1,0:T(8,128)}, u32[]{:S(2)}) copy-start(f32[4,253,128]{2,1,0:T(8,128)} %get-tuple-element.226) | copy-start | bytes 1554436
  24.0 1.3 %copy-start.3 = (f32[4,253,128]{2,1,0:T(8,128)S(1)}, f32[4,253,128]{2,1,0:T(8,128)}, u32[]{:S(2)}) copy-start(f32[4,253,128]{2,1,0:T(8,128)} %get-tuple-element.227) | copy-start | bytes 1554436
where the time goes:
time: 55.1 us; the launch traced here: 54.8 us
  blocking collectives  19.3 us (35%)
  local copies, waits for them, and re-layouts  12.8 us (23%)
  starting transfers between devices  12.4 us (23%)
  other arithmetic  9.54 us (17%)
  between operations  0.83 us (2%)
    all_gather x1, blocking collectives, shards(): gathered = lax.all_gather(stacked, 'gx', axis=1, tiled=True)  19.3 us
    ppermute x2, starting transfers between devices, padded_2(): lax.ppermute(head, axis, [((i + 1) % count, i) for i in range(ends)])  8.41 us
    add x11, other arithmetic, combine_rows(): value + factor_low * lower_value + factor_high * upper_value  4.48 us
    ppermute x2, starting transfers between devices, padded_2(): lax.ppermute(tail, axis, [(i, (i + 1) % count) for i in range(ends)])  3.95 us
    unnamed x16, local copies, waits for them, and re-layouts  3.76 us
    slice x40, local copies, waits for them, and re-layouts, rows_below(): lax.slice_in_dim(values, 0, length - stride, axis=sweep_direction)  2.66 us
    slice x2, local copies, waits for them, and re-layouts, padded_2(): head = lax.slice_in_dim(cells, 0, width, axis=dim)  2.62 us
    slice x26, local copies, waits for them, and re-layouts, rows_above(): lax.slice_in_dim(values, stride, length, axis=sweep_direction)  2.09 us
  transfers between devices with their start and end apart: 4, of which 0 were waited for; matrix products, arithmetic and copies ran while one was open for 12% of the time, Pallas kernels for 0%

commit v1 on v0

--- a/solution.py
+++ b/solution.py
@@ -138,7 +138,9 @@
     reduced_super = jnp.concatenate([super_first, super_last], 1)
     reduced_right = jnp.concatenate([right_first, right_last], 1)
     stacked = jnp.concatenate([reduced_sub, reduced_diag, reduced_super, reduced_right], 1)
-    gathered = lax.all_gather(stacked, "gx", axis=1, tiled=True)
+    gathered = jnp.concatenate(
+        lax.all_to_all(jnp.stack([stacked] * lax.axis_size("gx")), "gx", 0, 0), axis=1
+    )
     gathered = gathered.reshape(gathered.shape[0], device_count, 4, 2, gathered.shape[-1])
     gathered_lower_band, gathered_diagonal, gathered_upper_band, gathered_rhs = (
         gathered[:, :, k].reshape(gathered.shape[0], 2 * device_count, gathered.shape[-1])

time: 55.1 us -> 55 us (level)
  blocking collectives: 19.3 us -> 0 us
  waiting for transfers between devices: 0.01 us -> 11.6 us
  starting transfers between devices: 12.4 us -> 19.9 us
    all_gather x1 -> x0, blocking collectives: 19.3 us -> none  [shards(): gathered = lax.all_gather(stacked, 'gx', axis=1, tiled=True)]
    all_to_all x0 -> x1, waiting for transfers between devices: none -> 11.6 us  [shards(): lax.all_to_all(jnp.stack([stacked] * lax.axis_size('gx')), 'gx', 0, 0)]
    all_to_all x0 -> x1, starting transfers between devices: none -> 7.53 us  [shards(): lax.all_to_all(jnp.stack([stacked] * lax.axis_size('gx')), 'gx', 0, 0)]
    slice x26, local copies, waits for them, and re-layouts: 2.09 us -> 1.1 us  [rows_above(): lax.slice_in_dim(values, stride, length, axis=sweep_direction)]
    another operation x0 -> x1, local copies, waits for them, and re-layouts: none -> 0.73 us  [shards(): jnp.stack([stacked] * lax.axis_size('gx'))]
    unnamed x16 -> x12, local copies, waits for them, and re-layouts: 3.76 us -> 3.65 us
  transfers between devices with their start and end apart: 4 -> 5, of which waited for: 0 -> 1; matrix products, arithmetic and copies ran while one was open for 12% -> 10% of each run, Pallas kernels for 0% -> 0%
where the time goes in v1:
time: 55 us; the launch traced here: 54.5 us
  starting transfers between devices  19.9 us (36%)
  local copies, waits for them, and re-layouts  12.6 us (23%)
  waiting for transfers between devices  11.6 us (21%)
  other arithmetic  9.56 us (17%)
  between operations  0.84 us (2%)
    all_to_all x1, waiting for transfers between devices, shards(): lax.all_to_all(jnp.stack([stacked] * lax.axis_size('gx')), 'gx', 0, 0)  11.6 us
    ppermute x2, starting transfers between devices, padded_2(): lax.ppermute(head, axis, [((i + 1) % count, i) for i in range(ends)])  8.41 us
    all_to_all x1, starting transfers between devices, shards(): lax.all_to_all(jnp.stack([stacked] * lax.axis_size('gx')), 'gx', 0, 0)  7.53 us
    add x11, other arithmetic, combine_rows(): value + factor_low * lower_value + factor_high * upper_value  4.5 us
    ppermute x2, starting transfers between devices, padded_2(): lax.ppermute(tail, axis, [(i, (i + 1) % count) for i in range(ends)])  3.95 us
    unnamed x12, local copies, waits for them, and re-layouts  3.65 us
    slice x40, local copies, waits for them, and re-layouts, rows_below(): lax.slice_in_dim(values, 0, length - stride, axis=sweep_direction)  2.66 us
    slice x2, local copies, waits for them, and re-layouts, padded_2(): head = lax.slice_in_dim(cells, 0, width, axis=dim)  2.62 us
  transfers between devices with their start and end apart: 5, of which 1 were waited for; matrix products, arithmetic and copies ran while one was open for 10% of the time, Pallas kernels for 0%

profile of v1, /device:TPU:1, one launch (start us, length us, event | category | flops | bytes accessed | tf_op | source)
XLA Modules:
  0.0 54.5 jit_solution(15803460261263326386)
XLA Ops:
  0.0 1.9 %fusion.76 = (f32[2,256,128]{2,1,0:T(8,128)}, f32[2,256,128]{2,1,0:T(8,128)}) fusion(f32[4,256,128]{2,1,0:T(8,128)} %param.3), kind=kLoop, calls=%fused_computation.204 | loop fusion | bytes 1048576 | tf_op jit(solution)/shard_map/slice | solution.py:11
  1.9 2.0 %collective-permute-start.3 = (f32[2,256,128]{2,1,0:T(8,128)}, f32[2,256,128]{2,1,0:T(8,128)}, u32[]{:S(2)}, u32[]{:S(2)}) collective-permute-start(f32[2,256,128]{2,1,0:T(8,128)} %get-tuple-element.169), channel_id=1, source_target_pairs={{0,1},{1,2},{2,3},{3,4},{4,5},{5,6},{6,7},{7,8},{8,9},{9,10},{10,1... | collective-permute-start | bytes 786440 | tf_op jit(solution)/shard_map/ppermute | solution.py:15
  3.9 3.7 %collective-permute-start.2 = (f32[2,256,128]{2,1,0:T(8,128)}, f32[2,256,128]{2,1,0:T(8,128)S(1)}, u32[]{:S(2)}, u32[]{:S(2)}) collective-permute-start(f32[2,256,128]{2,1,0:T(8,128)} %get-tuple-element.168), channel_id=1, source_target_pairs={{1,0},{2,1},{3,2},{4,3},{5,4},{6,5},{7,6},{8,7},{9,8},{10,9},{11,1... | collective-permute-start | bytes 786440 | tf_op jit(solution)/shard_map/ppermute | solution.py:17
  7.6 0.7 %fusion.78 = (f32[4,2,128]{2,1,0:T(2,128)S(1)}, f32[4,2,128]{2,1,0:T(2,128)S(1)}) fusion(f32[4,256,128]{2,1,0:T(8,128)} %param.3), kind=kLoop, calls=%fused_computation.206 | loop fusion | bytes 16384 | tf_op jit(solution)/shard_map/slice | solution.py:11
  8.4 4.7 %collective-permute-start = (f32[4,2,128]{2,1,0:T(2,128)S(1)}, f32[4,2,128]{2,1,0:T(2,128)S(1)}, u32[]{:S(2)}, u32[]{:S(2)}) collective-permute-start(f32[4,2,128]{2,1,0:T(2,128)S(1)} %get-tuple-element.175), channel_id=1, source_target_pairs={{16,0},{32,16},{48,32},{64,48},{80,64},{96,80},{112,96},{128,112},... | collective-permute-start | bytes 12296 | tf_op jit(solution)/shard_map/ppermute | solution.py:17
  13.1 1.9 %collective-permute-start.1 = (f32[4,2,128]{2,1,0:T(2,128)S(1)}, f32[4,2,128]{2,1,0:T(2,128)S(1)}, u32[]{:S(2)}, u32[]{:S(2)}) collective-permute-start(f32[4,2,128]{2,1,0:T(2,128)S(1)} %get-tuple-element.176), channel_id=1, source_target_pairs={{0,16},{16,32},{32,48},{48,64},{64,80},{80,96},{96,112},{112,128},... | collective-permute-start | bytes 12296 | tf_op jit(solution)/shard_map/ppermute | solution.py:15
  15.0 1.1 %multiply_add_fusion.26 = (f32[4,256,128]{2,1,0:T(8,128)S(1)}, f32[4,256,128]{2,1,0:T(8,128)S(1)}) fusion(f32[4,256,128]{2,1,0:T(8,128)} %param.5), kind=kLoop, calls=%fused_computation.95 | loop fusion | flops 393216 | bytes 1572864 | tf_op jit(solution)/shard_map/add | solution.py:114
  16.1 1.2 %fusion.73 = (f32[4,253,128]{2,1,0:T(8,128)S(1)}, f32[4,253,128]{2,1,0:T(8,128)S(1)}, f32[4,253,128]{2,1,0:T(8,128)}, f32[4,253,128]{2,1,0:T(8,128)}) fusion(f32[4,256,128]{2,1,0:T(8,128)S(1)} %get-tuple-element.165, f32[4,256,128]{2,1,0:T(8,128)S(1)} %get-tuple-element.164), kind=kLoop, calls=%fused_computation.201 | loop fusion | bytes 4145152 | tf_op jit(solution)/shard_map/slice | solution.py:119
  17.4 0.8 %pad_slice_fusion.9 = f32[4,253,128]{2,1,0:T(8,128)} fusion(f32[4,253,128]{2,1,0:T(8,128)S(1)} %get-tuple-element.161), kind=kLoop, calls=%fused_computation.97 | loop fusion | bytes 1036288 | tf_op jit(solution)/shard_map/slice | solution.py:49
  18.7 1.1 %constant_dynamic-update-slice_fusion.5 = f32[6,256,128]{2,1,0:T(8,128)S(1)} fusion(f32[2,256,128]{2,1,0:T(8,128)} %collective-permute-done.3), kind=kLoop, calls=%fused_computation.133 | loop fusion | bytes 524288
  20.2 1.2 %fusion.10 = f32[4,256,128]{2,1,0:T(8,128)S(1)} fusion(f32[4,256,128]{2,1,0:T(8,128)S(1)} %copy-done, f32[4,2,128]{2,1,0:T(2,128)S(1)} %collective-permute-done.1, f32[4,258,128]{2,1,0:T(8,128)S(1)} %constant_dynamic-update-slice_fusion, f32[4,256,2]{2,1,0:T(8,128)S(1)} %get-tuple-element.174, f32[4,256,2]{2,1,0:T(8,128)S(1)} %get-tuple-element.173, ...), kind=kLoop, calls=%fused_computation.20 | loop fusion | flops 6029312 | bytes 5787648 | tf_op jit(solution)/shard_map/add | solution.py:42
  21.5 0.9 %copy-done.2 = f32[4,253,128]{2,1,0:T(8,128)S(1)} copy-done((f32[4,253,128]{2,1,0:T(8,128)S(1)}, f32[4,253,128]{2,1,0:T(8,128)}, u32[]{:S(2)}) %copy-start.2) | copy-done | bytes 518168
  23.3 1.0 %copy-done.1 = f32[4,253,128]{2,1,0:T(8,128)S(1)} copy-done((f32[4,253,128]{2,1,0:T(8,128)S(1)}, f32[4,253,128]{2,1,0:T(8,128)}, u32[]{:S(2)}) %copy-start.1) | copy-done | bytes 518168
  24.2 0.6 %multiply_add_fusion.6 = (f32[4,254,128]{2,1,0:T(8,128)S(1)}, f32[4,254,128]{2,1,0:T(8,128)S(1)}, f32[4,254,128]{2,1,0:T(8,128)S(1)}, f32[4,254,128]{2,1,0:T(8,1...) fusion(f32[4,252,128]{2,1,0:T(8,128)S(1)} %get-tuple-element.159, ...), kind=kLoop, calls=%fused_computation.43 | loop fusion | flops 2340864 | bytes 9343992 | tf_op jit(solution)/shard_map/add | solution.py:75
  25.4 0.9 %multiply_add_fusion.5 = (f32[4,254,128]{2,1,0:T(8,128)S(1)}, f32[4,254,128]{2,1,0:T(8,128)S(1)}, f32[4,254,128]{2,1,0:T(8,128)S(1)}, f32[4,254,128]{2,1,0:T(8,1...) fusion(f32[4,250,128]{2,1,0:T(8,128)S(1)} %get-tuple-element.155, ...), kind=kLoop, calls=%fused_computation.42 | loop fusion | flops 2340864 | bytes 11386880 | tf_op jit(solution)/shard_map/add | solution.py:75
  26.9 0.7 %multiply_add_fusion.4 = (f32[4,254,128]{2,1,0:T(8,128)S(1)}, f32[4,254,128]{2,1,0:T(8,128)S(1)}, f32[4,254,128]{2,1,0:T(8,128)S(1)}, f32[4,254,128]{2,1,0:T(8,1...) fusion(f32[4,246,128]{2,1,0:T(8,128)S(1)} %get-tuple-element.147, ...), kind=kLoop, calls=%fused_computation.41 | loop fusion | flops 2340864 | bytes 11329536 | tf_op jit(solution)/shard_map/add | solution.py:75
  28.2 0.4 multiply_add_fusion.3
  29.2 0.5 multiply_add_fusion.2
  30.3 0.5 multiply_add_fusion.1
  31.0 0.4 multiply_add_fusion.7
  32.5 0.7 %stack.2 = f32[16,4,8,128]{3,2,1,0:T(8,128)} broadcast(f32[4,8,128]{2,1,0:T(8,128)S(1)} %concatenate.548), dimensions={1,2,3} | broadcast | bytes 278528 | tf_op jit(solution)/shard_map/stack | solution.py:142
  33.2 7.5 %all-to-all-start = ((f32[16,4,8,128]{3,2,1,0:T(8,128)}), f32[16,4,8,128]{3,2,1,0:T(8,128)S(1)}, u32[]{:S(2)}, u32[]{:S(2)}) async-start(f32[16,4,8,128]{3,2,1,0:T(8,128)} %stack.2), calls=%async_computation | async-start | bytes 524288 | tf_op jit(solution)/shard_map/all_to_all | solution.py:142
  40.7 11.6 %all-to-all-done = f32[16,4,8,128]{3,2,1,0:T(8,128)S(1)} async-done(((f32[16,4,8,128]{3,2,1,0:T(8,128)}), f32[16,4,8,128]{3,2,1,0:T(8,128)S(1)}, u32[]{:S(2)}, u32[]{:S(2)}) %all-to-all-start) | async-done | bytes 262176 | tf_op jit(solution)/shard_map/all_to_all | solution.py:142
  53.6 0.8 %pad_maximum_fusion.3 = f32[4,256,128]{2,1,0:T(8,128)} fusion(f32[4,1,128]{2,1,0:T(1,128)S(1)} %get-tuple-element.223, f32[4,254,128]{2,1,0:T(8,128)S(1)} %multiply_add_fusion, f32[4,1,128]{2,1,0:T(1,128)S(1)} %get-tuple-element.222), kind=kLoop, calls=%fused_computation.33 | loop fusion | flops 262144 | bytes 1048576 | tf_op jit(solution)/shard_map/concatenate | solution.py:156
  (111 shorter events, 6.7 us)
Async XLA Ops:
  1.9 16.9 %collective-permute-start.3 = (f32[2,256,128]{2,1,0:T(8,128)}, f32[2,256,128]{2,1,0:T(8,128)}, u32[]{:S(2)}, u32[]{:S(2)}) collective-permute-start(f32[2,256,128]{2,1,0:T(8,128)} %get-tuple-element.169), channel_id=1, source_target_pairs={{0,1},{1,2},{2,3},{3,4},{4,5},{5,6},{6,7},{7,8},{8,9},{9,10},{10,1... | collective-permute-start | bytes 786440 | tf_op jit(solution)/shard_map/ppermute | solution.py:15
  3.9 16.0 %collective-permute-start.2 = (f32[2,256,128]{2,1,0:T(8,128)}, f32[2,256,128]{2,1,0:T(8,128)S(1)}, u32[]{:S(2)}, u32[]{:S(2)}) collective-permute-start(f32[2,256,128]{2,1,0:T(8,128)} %get-tuple-element.168), channel_id=1, source_target_pairs={{1,0},{2,1},{3,2},{4,3},{5,4},{6,5},{7,6},{8,7},{9,8},{10,9},{11,1... | collective-permute-start | bytes 786440 | tf_op jit(solution)/shard_map/ppermute | solution.py:17
  8.4 11.6 %collective-permute-start = (f32[4,2,128]{2,1,0:T(2,128)S(1)}, f32[4,2,128]{2,1,0:T(2,128)S(1)}, u32[]{:S(2)}, u32[]{:S(2)}) collective-permute-start(f32[4,2,128]{2,1,0:T(2,128)S(1)} %get-tuple-element.175), channel_id=1, source_target_pairs={{16,0},{32,16},{48,32},{64,48},{80,64},{96,80},{112,96},{128,112},... | collective-permute-start | bytes 12296 | tf_op jit(solution)/shard_map/ppermute | solution.py:17
  13.1 6.9 %collective-permute-start.1 = (f32[4,2,128]{2,1,0:T(2,128)S(1)}, f32[4,2,128]{2,1,0:T(2,128)S(1)}, u32[]{:S(2)}, u32[]{:S(2)}) collective-permute-start(f32[4,2,128]{2,1,0:T(2,128)S(1)} %get-tuple-element.176), channel_id=1, source_target_pairs={{0,16},{16,32},{32,48},{48,64},{64,80},{80,96},{96,112},{112,128},... | collective-permute-start | bytes 12296 | tf_op jit(solution)/shard_map/ppermute | solution.py:15
  17.4 1.2 %copy-start = (f32[4,256,128]{2,1,0:T(8,128)S(1)}, f32[4,256,128]{2,1,0:T(8,128)}, u32[]{:S(2)}) copy-start(f32[4,256,128]{2,1,0:T(8,128)} %param.3) | copy-start | bytes 1572868
  18.7 1.5 %copy-start.4 = (f32[3,4,256,128]{3,2,1,0:T(8,128)S(1)}, f32[3,4,256,128]{3,2,1,0:T(8,128)}, u32[]{:S(2)}) copy-start(f32[3,4,256,128]{3,2,1,0:T(8,128)} %param.4) | copy-start | bytes 4718596
  21.4 1.0 %copy-start.2 = (f32[4,253,128]{2,1,0:T(8,128)S(1)}, f32[4,253,128]{2,1,0:T(8,128)}, u32[]{:S(2)}) copy-start(f32[4,253,128]{2,1,0:T(8,128)} %get-tuple-element.224) | copy-start | bytes 1554436
  21.4 1.2 %copy-start.3 = (f32[4,253,128]{2,1,0:T(8,128)S(1)}, f32[4,253,128]{2,1,0:T(8,128)}, u32[]{:S(2)}) copy-start(f32[4,253,128]{2,1,0:T(8,128)} %get-tuple-element.225) | copy-start | bytes 1554436
  23.2 1.0 %copy-start.1 = (f32[4,253,128]{2,1,0:T(8,128)S(1)}, f32[4,253,128]{2,1,0:T(8,128)}, u32[]{:S(2)}) copy-start(f32[4,253,128]{2,1,0:T(8,128)} %pad_slice_fusion.9) | copy-start | bytes 1554436
  33.2 19.1 %all-to-all-start = ((f32[16,4,8,128]{3,2,1,0:T(8,128)}), f32[16,4,8,128]{3,2,1,0:T(8,128)S(1)}, u32[]{:S(2)}, u32[]{:S(2)}) async-start(f32[16,4,8,128]{3,2,1,0:T(8,128)} %stack.2), calls=%async_computation | async-start | bytes 524288 | tf_op jit(solution)/shard_map/all_to_all | solution.py:142
